TPU v7x, 256 devices: a whole 4x4x8 slice. The times are simulated.
256 devices in a mesh: tm: 4 (over y), row: 4 (over x), col: 16 (over z, core).
Axes of the slice: x: 4, y: 4, z: 8, core: 2. Of those that a mesh axis runs over, the one named last changes fastest.
Arguments:
- day_block: float32 [4, 4, 16, 32, 4, 4, 128], P('tm', None, 'col', None, None, 'row'), as said below
- left_coupling: float32 [4, 4, 16, 32, 4, 4, 128], P('tm', None, 'col', None, None, 'row'), may hold values from -0.125 to 0.125
- right_coupling: float32 [4, 4, 16, 32, 4, 4, 128], P('tm', None, 'col', None, None, 'row'), may hold values from -0.125 to 0.125
- separator_block: float32 [4, 4, 16, 32, 4, 4, 128], P('tm', None, 'col', None, None, 'row')
- arrow_coupling: float32 [4, 4, 16, 32, 64], P('tm', None, 'col'), may hold values from -0.125 to 0.125
- arrow_block: float32 [64, 64], replicated
Outputs:
- day_factor: float32 [4, 4, 16, 32, 4, 4, 128], P('tm', None, 'col', None, None, 'row')
- left_factor: float32 [4, 4, 16, 32, 4, 4, 128], P('tm', None, 'col', None, None, 'row')
- right_factor: float32 [4, 4, 16, 32, 4, 4, 128], P('tm', None, 'col', None, None, 'row')
- arrow_factor: float32 [4, 4, 16, 32, 64], P('tm', None, 'col')
- separator: float32 [4, 4, 16, 32, 4, 4, 128], P('tm', None, 'col', None, None, 'row')
- arrowhead: float32 [64, 64], replicated
Inputs may be any that keep to these rules, and one draw needn't show every extreme that they name: Each group's day_block and separator_block, and arrow_block, is an exactly symmetric matrix with all eigenvalues at least 1.
All inputs are finite; a program needn't handle non-finite values.
Results may differ from a plain program's by a relative error of at most 0.0001.
Values sent between devices are 32-bit elements; how exact they have to be, the bound alone decides.
No kernel may reach another device: no remote copies, remote signals or barrier semaphores. Data moves between devices by JAX's collectives and lax.ppermute only.
A program may use at most 128 MiB of HBM per device.

v0:
```python
import jax
import jax.numpy as jnp
from jax import lax
from jax.sharding import PartitionSpec as P


def passed_along(value, axis, steps):
    count = lax.axis_size(axis)
    initial, last = (max(0, -steps), min(count, count - steps))
    return lax.ppermute(value, axis, [(source, source + steps) for source in range(initial, last)])


def product(left, right):
    return jnp.dot(left, right, precision=lax.Precision.HIGHEST, preferred_element_type=jnp.float32)


def lower_inverse(factor):
    identity = jnp.eye(factor.shape[0], dtype=jnp.float32)
    return lax.linalg.triangular_solve(factor, identity, left_side=True, lower=True)


def reorder_nodes(whole, panels, col_width):
    count = whole.shape[0]
    col_count = lax.axis_size("col")
    spread = whole.reshape(count, panels, col_count, col_width)
    return jnp.transpose(spread, (2, 1, 3, 0)).reshape(col_count * panels * col_width, count)


def separator_term(solved, panels, col_width, row_width):
    whole = lax.all_gather(
        solved.reshape(solved.shape[0], panels, 1, row_width), "row", axis=2, tiled=True
    )
    ordered = reorder_nodes(whole, panels, col_width)
    return lax.psum_scatter(product(ordered, solved), "col", scatter_dimension=0, tiled=True)


def product_tn(left, right):
    return lax.dot_general(
        left,
        right,
        (((0,), (0,)), ((), ())),
        precision=lax.Precision.HIGHEST,
        preferred_element_type=jnp.float32,
    )


def per_device(
    day_block, left_coupling, right_coupling, separator_block, arrow_coupling, arrow_block
):
    panels = day_block.shape[1]
    col_width = day_block.shape[3]
    row_width = day_block.shape[6]
    col_count = lax.axis_size("col")
    row_count = lax.axis_size("row")
    panel_size = col_width * col_count
    arrow_rows = arrow_block.shape[0]
    col_index = lax.axis_index("col")
    row_index = lax.axis_index("row")
    matrix = day_block.reshape(panels, col_width, panels, row_width)
    left_part = left_coupling.reshape(panels, col_width, panels * row_width)
    right_part = right_coupling.reshape(panels, col_width, panels * row_width)
    arrow_part = arrow_coupling.reshape(panels, col_width, arrow_rows)

    def gather_block_row(k, after):
        piece = matrix[k, :, k:, :]
        if after is not None:
            piece, _ = lax.optimization_barrier((piece, after))
        by_col = lax.all_gather(piece, "col", axis=0, tiled=True)
        whole = lax.all_gather(by_col[:, :, None, :], "row", axis=2, tiled=True)
        return whole.reshape(panel_size, (panels - k) * panel_size)

    def gather_coupling(k, after):
        pieces = (left_part[k], right_part[k])
        if after is not None:
            pieces, _ = lax.optimization_barrier((pieces, after))
        return tuple((lax.all_gather(piece, "col", axis=0, tiled=True) for piece in pieces))

    block_rows = [gather_block_row(0, None)] + [None] * (panels - 1)
    left_full = [None] * panels
    right_full = [None] * panels
    left_full[0], right_full[0] = gather_coupling(0, None)
    arrow_all = lax.all_gather(arrow_part, "col", axis=1, tiled=True)
    arrow_full = [arrow_all[k] for k in range(panels)]
    pending = [[] for _ in range(panels)]
    pending_left = [[] for _ in range(panels)]
    pending_right = [[] for _ in range(panels)]
    rows_at = col_index * col_width + lax.broadcasted_iota(jnp.int32, (col_width, row_width), 0)
    cols_at = row_index * row_width + lax.broadcasted_iota(jnp.int32, (col_width, row_width), 1)
    per_slice = row_width // col_width
    owner = col_index // per_slice
    offset = col_index % per_slice * col_width

    def own_columns(solved):
        spread = solved.reshape(panel_size, panels, row_width)
        picked = lax.dynamic_slice_in_dim(spread, offset, col_width, 2)
        picked = jnp.where(row_index == owner, picked, 0.0)
        return lax.psum(picked, "row").reshape(panel_size, panels * col_width)

    factor_blocks = []
    left_solved = []
    right_solved = []
    arrow_solved = []
    right_term = jnp.zeros((panels * col_width, panels * row_width), jnp.float32)
    left_term = jnp.zeros((panels * col_width, panels * row_width), jnp.float32)
    arrow_term = jnp.zeros((arrow_rows, arrow_rows), jnp.float32)
    for current in range(panels):
        remain = panels - current
        block_row = block_rows[current]
        for update in pending[current]:
            block_row = block_row - update
        diagonal_full = block_row[:, :panel_size]
        factor = jnp.linalg.cholesky(diagonal_full)
        if remain > 1:
            block_rows[current + 1] = gather_block_row(current + 1, factor)
            fresh_left, fresh_right = gather_coupling(current + 1, factor)
            for update in pending_left[current + 1]:
                fresh_left = fresh_left - update
            for update in pending_right[current + 1]:
                fresh_right = fresh_right - update
            left_full[current + 1], right_full[current + 1] = (fresh_left, fresh_right)
        inverse = lower_inverse(factor)
        owned_full = product(inverse, block_row)
        owned = lax.dynamic_slice_in_dim(
            owned_full.reshape(panel_size, remain, row_count, row_width), row_index, 1, 2
        ).reshape(panel_size, remain, row_width)
        solved_left = product(inverse, left_full[current])
        solved_right = product(inverse, right_full[current])
        solved_arrow = product(inverse, arrow_full[current])
        left_solved.append(solved_left)
        right_solved.append(solved_right)
        arrow_solved.append(solved_arrow)
        right_term = right_term + product_tn(own_columns(solved_right), solved_right)
        left_term = left_term + product_tn(own_columns(solved_left), solved_left)
        arrow_term = arrow_term + product_tn(solved_arrow, solved_arrow)
        mine_rows = lax.dynamic_slice_in_dim(owned, col_index * col_width, col_width, 0)
        diagonal_part = jnp.where(cols_at >= rows_at, mine_rows[:, 0, :], 0.0)
        factor_blocks.append(
            jnp.concatenate(
                [
                    jnp.zeros((col_width, current, row_width), jnp.float32),
                    diagonal_part[:, None, :],
                    mine_rows[:, 1:, :],
                ],
                axis=1,
            )
        )
        if remain > 1:
            later = owned_full[:, panel_size:]
            for step in range(remain - 1):
                target = current + 1 + step
                rows = slice(step * panel_size, (step + 1) * panel_size)
                pending[target].append(product_tn(later[:, rows], later[:, step * panel_size :]))
            left_update = product_tn(later, solved_left)
            right_update = product_tn(later, solved_right)
            arrow_update = product_tn(later, solved_arrow)
            for step in range(remain - 1):
                rows = slice(step * panel_size, (step + 1) * panel_size)
                target = current + 1 + step
                if step == 0:
                    left_full[target] = left_full[target] - left_update[rows]
                    right_full[target] = right_full[target] - right_update[rows]
                else:
                    pending_left[target].append(left_update[rows])
                    pending_right[target].append(right_update[rows])
                arrow_full[target] = arrow_full[target] - arrow_update[rows]
    day_factor = jnp.stack(factor_blocks).reshape(day_block.shape)

    def mine(parts, width):
        whole = jnp.stack(parts).reshape(panels, col_count, col_width, width)
        return lax.dynamic_index_in_dim(whole, col_index, 1, keepdims=False)

    left_out = mine(left_solved, panels * row_width)
    right_out = mine(right_solved, panels * row_width)
    arrow_out = mine(arrow_solved, arrow_rows)
    separator_local = separator_block.reshape(panels * col_width, panels * row_width)
    from_next = passed_along(left_term, "tm", -1)
    separator = separator_local - right_term - from_next
    arrow_total = jnp.sum(lax.all_gather(arrow_term, "tm", axis=0, tiled=False), axis=0)
    arrowhead = arrow_block - arrow_total
    return (
        day_factor,
        left_out.reshape(left_coupling.shape),
        right_out.reshape(right_coupling.shape),
        arrow_out.reshape(arrow_coupling.shape),
        separator.reshape(separator_block.shape),
        arrowhead,
    )


def solution(mesh):
    return jax.shard_map(
        per_device,
        mesh=mesh,
        in_specs=(
            P("tm", None, "col", None, None, "row", None),
            P("tm", None, "col", None, None, "row", None),
            P("tm", None, "col", None, None, "row", None),
            P("tm", None, "col", None, None, "row", None),
            P("tm", None, "col", None, None),
            P(),
        ),
        out_specs=(
            P("tm", None, "col", None, None, "row", None),
            P("tm", None, "col", None, None, "row", None),
            P("tm", None, "col", None, None, "row", None),
            P("tm", None, "col", None, None),
            P("tm", None, "col", None, None, "row", None),
            P(),
        ),
        check_vma=False,
    )
```

profile of v0, /device:TPU:8, one launch (start us, length us, event | category | flops | bytes accessed | tf_op | source)
XLA Modules:
  0.0 1049.3 jit_solution(13707844531146109400)
XLA Ops:
  8.9 43.0 %all-gather.37.cloned.1.call-done = f32[1,1,1,512,4,1,128]{6,4,5,2,1,0,3:T(4,128)} async-done(((f32[1,1,1,32,4,1,128]{6,4,5,2,1,0,3:T(4,128)}), f32[1,1,1,512,4,1,128]{6,4,5,2,1,0,3:T(4,128)}) %all-gather.37.cloned.1.call-update) | async-done | bytes 1048592 | tf_op jit(solution)/shard_map/all_gather | solution.py:68
  57.8 18.4 %all-gather.5 = f32[1,4,1,512,64]{4,1,2,0,3:T(4,128)S(1)} all-gather(f32[1,4,1,32,64]{4,1,2,0,3:T(4,128)S(1)} %copy.85), channel_id=7, replica_groups=mesh['tm'=4,'row'=4,'col'=16] {'col'}, dimensions={3}, use_global_device_ids=true | all-gather | bytes 557056 | tf_op jit(solution)/shard_map/all_gather | solution.py:82
  76.9 26.8 %all-gather.39.cloned.1.call-done = f32[1,1,1,512,4,4,128]{6,3,4,2,1,0,5:T(8,128)} async-done(((f32[1,1,1,512,4,1,128]{6,3,4,2,1,0,5:T(8,128)}), f32[1,1,1,512,4,4,128]{6,3,4,2,1,0,5:T(8,128)}) %all-gather.39.cloned.1.call-update) | async-done | bytes 4194320 | tf_op jit(solution)/shard_map/all_gather | solution.py:69
  103.6 5.5 copy.65
  112.2 11.7 %cholesky.462 = f32[128,128]{1,0:T(8,128)S(1)} custom-call(f32[128,128]{1,0:T(8,128)S(1)} %cholesky.746), custom_call_target="Cholesky" | custom-call | tf_op jit(solution)/shard_map/jit(cholesky)/cholesky | solution.py:112
  124.0 9.8 custom-call.35
  135.2 12.5 %cholesky.481 = f32[128,128]{1,0:T(8,128)S(1)} custom-call(f32[128,128]{1,0:T(8,128)} %cholesky.750), custom_call_target="Cholesky" | custom-call | tf_op jit(solution)/shard_map/jit(cholesky)/cholesky | solution.py:112
  148.4 11.1 %custom-call.36 = f32[1,128,128]{1,2,0:T(8,128)S(1)} custom-call(f32[1,128,128]{2,1,0:T(8,128)} %get-tuple-element.176), custom_call_target="InvertDiagBlocksLowerTriangular" | custom-call | tf_op jit(solution)/shard_map/jit(cholesky)/cholesky | solution.py:112
  160.3 11.7 %cholesky.502 = f32[128,128]{1,0:T(8,128)S(1)} custom-call(f32[128,128]{1,0:T(8,128)S(1)} %cholesky.755), custom_call_target="Cholesky" | custom-call | tf_op jit(solution)/shard_map/jit(cholesky)/cholesky | solution.py:112
  172.0 9.8 custom-call.37
  182.4 11.7 %cholesky.519 = f32[128,128]{1,0:T(8,128)S(1)} custom-call(f32[128,128]{1,0:T(8,128)S(1)} %convolution_subtract_fusion.30), custom_call_target="Cholesky" | custom-call | tf_op jit(solution)/shard_map/jit(cholesky)/cholesky | solution.py:112
  199.0 21.4 %all_gather.59 = f32[512,3,128]{2,0,1:T(8,128)} all-gather(f32[32,3,128]{2,0,1:T(8,128)} %slice_bitcast_fusion.32), channel_id=1, replica_groups=mesh['tm'=4,'row'=4,'col'=16] {'col'}, dimensions={0}, use_global_device_ids=true | all-gather | bytes 835584 | tf_op jit(solution)/shard_map/all_gather | solution.py:68
  230.8 8.0 while.8
  238.9 39.3 %custom-call.38 = f32[4,128,128]{1,2,0:T(8,128)S(1)} custom-call(f32[4,128,128]{2,1,0:T(8,128)S(1)} %get-tuple-element.52), custom_call_target="InvertDiagBlocksLowerTriangular" | custom-call | tf_op jit(solution)/shard_map/triangular_solve/custom-call.3 | solution.py:19
  283.3 8.6 fusion.183
  291.9 6.2 reshape.296
  314.0 4.8 fusion
  318.8 4.9 fusion.7
  323.7 7.6 fusion.2
  331.2 7.1 fusion.4
  341.9 7.8 convolution_subtract_fusion
  356.2 11.7 %cholesky.534 = f32[128,128]{1,0:T(8,128)S(1)} custom-call(f32[128,128]{1,0:T(8,128)S(1)} %cholesky.759), custom_call_target="Cholesky" | custom-call | tf_op jit(solution)/shard_map/jit(cholesky)/cholesky | solution.py:112
  368.1 9.8 custom-call.39
  380.4 11.7 %cholesky.553 = f32[128,128]{1,0:T(8,128)S(1)} custom-call(f32[128,128]{1,0:T(8,128)S(1)} %cholesky.763), custom_call_target="Cholesky" | custom-call | tf_op jit(solution)/shard_map/jit(cholesky)/cholesky | solution.py:112
  392.1 10.2 custom-call.40
  403.9 11.7 %cholesky.574 = f32[128,128]{1,0:T(8,128)S(1)} custom-call(f32[128,128]{1,0:T(8,128)S(1)} %cholesky.768), custom_call_target="Cholesky" | custom-call | tf_op jit(solution)/shard_map/jit(cholesky)/cholesky | solution.py:112
  415.7 9.8 custom-call.41
  427.0 11.7 %cholesky.591 = f32[128,128]{1,0:T(8,128)S(1)} custom-call(f32[128,128]{1,0:T(8,128)S(1)} %convolution_subtract_fusion.29), custom_call_target="Cholesky" | custom-call | tf_op jit(solution)/shard_map/jit(cholesky)/cholesky | solution.py:112
  444.2 17.9 %all_gather.61 = f32[512,2,128]{2,1,0:T(2,128)} all-gather(f32[32,2,128]{2,1,0:T(2,128)S(1)} %copy.73), channel_id=1, replica_groups=mesh['tm'=4,'row'=4,'col'=16] {'col'}, dimensions={0}, use_global_device_ids=true | all-gather | bytes 557056 | tf_op jit(solution)/shard_map/all_gather | solution.py:68
  462.1 8.0 while.9
  470.2 39.3 %custom-call.42 = f32[4,128,128]{1,2,0:T(8,128)S(1)} custom-call(f32[4,128,128]{2,1,0:T(8,128)S(1)} %get-tuple-element.53), custom_call_target="InvertDiagBlocksLowerTriangular" | custom-call | tf_op jit(solution)/shard_map/triangular_solve/custom-call.3 | solution.py:19
  527.5 7.4 fusion.179
  545.7 4.8 fusion.12
  550.5 4.8 fusion.14
  555.4 4.1 copy.74
  559.5 5.5 fusion.9
  572.8 11.7 %cholesky.606 = f32[128,128]{1,0:T(8,128)S(1)} custom-call(f32[128,128]{1,0:T(8,128)S(1)} %cholesky.772), custom_call_target="Cholesky" | custom-call | tf_op jit(solution)/shard_map/jit(cholesky)/cholesky | solution.py:112
  585.7 9.8 custom-call.43
  598.7 11.7 %cholesky.625 = f32[128,128]{1,0:T(8,128)S(1)} custom-call(f32[128,128]{1,0:T(8,128)S(1)} %cholesky.776), custom_call_target="Cholesky" | custom-call | tf_op jit(solution)/shard_map/jit(cholesky)/cholesky | solution.py:112
  612.3 10.2 custom-call.44
  624.9 11.7 %cholesky.646 = f32[128,128]{1,0:T(8,128)S(1)} custom-call(f32[128,128]{1,0:T(8,128)S(1)} %cholesky.781), custom_call_target="Cholesky" | custom-call | tf_op jit(solution)/shard_map/jit(cholesky)/cholesky | solution.py:112
  637.2 9.8 custom-call.45
  649.3 11.7 %cholesky.663 = f32[128,128]{1,0:T(8,128)S(1)} custom-call(f32[128,128]{1,0:T(8,128)S(1)} %convolution_subtract_fusion.28), custom_call_target="Cholesky" | custom-call | tf_op jit(solution)/shard_map/jit(cholesky)/cholesky | solution.py:112
  668.1 11.6 %while.10 = (s32[]{:T(128)}, f32[512,512]{1,0:T(8,128)}, s32[4,2]{0,1:T(2,128)S(1)}, f32[4,128,128]{2,1,0:T(8,128)S(1)}, s32[]{:T(128)}) while((s32[]{:T(128)}, f32[512,512]{1,0:T(8,128)}, s32[4,2]{0,1:T(2,128)S(1)}, f32[4,128,128]{2,1,0:T(8,128)S(1)}, s32[]{:T(128)}) %tuple.178), condition=%wide.while_cond.clone.1, body=%wide.while_body.clone.1.sunk | while | flops 2 | bytes 131181 | solution.py:19
  679.7 39.9 %custom-call.46 = f32[4,128,128]{1,2,0:T(8,128)} custom-call(f32[4,128,128]{2,1,0:T(8,128)S(1)} %get-tuple-element.54), custom_call_target="InvertDiagBlocksLowerTriangular" | custom-call | tf_op jit(solution)/shard_map/triangular_solve/custom-call.3 | solution.py:19
  719.6 17.3 %all_gather.63 = f32[512,1,128]{2,0,1:T(8,128)} all-gather(f32[32,1,128]{2,0,1:T(8,128)S(1)} %copy-done.73), channel_id=1, replica_groups=mesh['tm'=4,'row'=4,'col'=16] {'col'}, dimensions={0}, use_global_device_ids=true | all-gather | bytes 278528 | tf_op jit(solution)/shard_map/all_gather | solution.py:68
  746.1 5.1 fusion.22
  753.8 5.0 fusion.24
  764.6 6.7 fusion.178
  786.8 3.9 convolution_subtract_fusion.5
  795.1 11.7 %cholesky.678 = f32[128,128]{1,0:T(8,128)S(1)} custom-call(f32[128,128]{1,0:T(8,128)S(1)} %cholesky.785), custom_call_target="Cholesky" | custom-call | tf_op jit(solution)/shard_map/jit(cholesky)/cholesky | solution.py:112
  807.0 10.0 custom-call.47
  818.7 11.7 %cholesky.697 = f32[128,128]{1,0:T(8,128)S(1)} custom-call(f32[128,128]{1,0:T(8,128)S(1)} %cholesky.789), custom_call_target="Cholesky" | custom-call | tf_op jit(solution)/shard_map/jit(cholesky)/cholesky | solution.py:112
  831.7 9.8 custom-call.48
  843.1 11.7 %cholesky.718 = f32[128,128]{1,0:T(8,128)S(1)} custom-call(f32[128,128]{1,0:T(8,128)S(1)} %cholesky.794), custom_call_target="Cholesky" | custom-call | tf_op jit(solution)/shard_map/jit(cholesky)/cholesky | solution.py:112
  855.5 10.0 custom-call.49
  866.9 11.7 %cholesky.735 = f32[128,128]{1,0:T(8,128)S(1)} custom-call(f32[128,128]{1,0:T(8,128)S(1)} %convolution_subtract_fusion.27), custom_call_target="Cholesky" | custom-call | tf_op jit(solution)/shard_map/jit(cholesky)/cholesky | solution.py:112
  883.0 11.6 %while.11 = (s32[]{:T(128)}, f32[512,512]{1,0:T(8,128)}, s32[4,2]{0,1:T(2,128)S(1)}, f32[4,128,128]{2,1,0:T(8,128)S(1)}, s32[]{:T(128)}) while((s32[]{:T(128)}, f32[512,512]{1,0:T(8,128)}, s32[4,2]{0,1:T(2,128)S(1)}, f32[4,128,128]{2,1,0:T(8,128)S(1)}, s32[]{:T(128)}) %tuple.179), condition=%wide.while_cond.clone.2, body=%wide.while_body.clone.2.sunk | while | flops 2 | bytes 131181 | solution.py:19
  894.6 40.3 %custom-call.50 = f32[4,128,128]{1,2,0:T(8,128)} custom-call(f32[4,128,128]{2,1,0:T(8,128)S(1)} %get-tuple-element.55), custom_call_target="InvertDiagBlocksLowerTriangular" | custom-call | tf_op jit(solution)/shard_map/triangular_solve/custom-call.3 | solution.py:19
  943.5 4.2 convolution_subtract_fusion.1
  954.9 3.9 convolution_subtract_fusion.2
  973.7 12.0 %all-gather.6 = f32[256,64]{1,0:T(8,128)S(1)} all-gather(f32[64,64]{1,0:T(8,128)S(1)} %convolution_add_fusion.6), channel_id=8, replica_groups=mesh['tm'=4,'row'=4,'col'=16] {'tm'}, dimensions={0}, use_global_device_ids=true | all-gather | bytes 81920 | tf_op jit(solution)/shard_map/all_gather | solution.py:178
  992.5 32.9 %all-reduce.5.cloned.1.call-done = (f32[512,128]{0,1:T(8,128)}, f32[512,128]{0,1:T(8,128)}, f32[512,128]{0,1:T(8,128)}, f32[512,128]{0,1:T(8,128)}, f32[512,128]...) async-done(((f32[512,128]{0,1:T(8,128)}, f32[512,128]{0,1:T(8,128)}, f32[512,128]{0,1:T(8,128)}, f32[512,128]{0,1:T(8,128)}, ...) | async-done | bytes 2097168 | tf_op jit(solution)/shard_map/psum | solution.py:97
  1035.2 5.8 collective-permute-done
  (461 shorter events, 252.1 us)
Async XLA Ops:
  7.2 50.6 %copy-start.50 = (f32[1,4,1,32,4,1,128]{6,5,4,3,2,1,0:T(1,128)S(1)}, f32[1,4,1,32,4,1,128]{6,5,4,3,2,1,0:T(1,128)}, u32[]{:S(2)}) copy-start(f32[1,4,1,32,4,1,128]{6,5,4,3,2,1,0:T(1,128)} %param.9) | copy-start | bytes 786436
  7.2 47.1 %copy-start.66 = (f32[1,4,1,32,4,1,128]{6,5,4,3,2,1,0:T(1,128)S(1)}, f32[1,4,1,32,4,1,128]{6,5,4,3,2,1,0:T(1,128)}, u32[]{:S(2)}) copy-start(f32[1,4,1,32,4,1,128]{6,5,4,3,2,1,0:T(1,128)} %param.10) | copy-start | bytes 786436
  7.2 47.1 %copy-start.65 = (f32[1,4,1,32,4,1,128]{6,5,4,3,2,1,0:T(1,128)S(1)}, f32[1,4,1,32,4,1,128]{6,5,4,3,2,1,0:T(1,128)}, u32[]{:S(2)}) copy-start(f32[1,4,1,32,4,1,128]{6,5,4,3,2,1,0:T(1,128)} %param.11) | copy-start | bytes 786436
  7.2 50.6 %copy-start.74 = (f32[1,4,1,32,64]{4,3,2,1,0:T(8,128)S(1)}, f32[1,4,1,32,64]{4,3,2,1,0:T(8,128)}, u32[]{:S(2)}) copy-start(f32[1,4,1,32,64]{4,3,2,1,0:T(8,128)} %param.13) | copy-start | bytes 98308
  7.2 44.7 %all-gather.37.cloned.1.call-start = ((), (), s32[]{:S(2)}) async-start(), calls=%async_computation.8 | async-start | bytes 1114112 | tf_op jit(solution)/shard_map/all_gather | solution.py:68
  8.8 94.8 %all-gather.39.cloned.1.call-start = ((), (), s32[]{:S(2)}) async-start(), calls=%async_computation.9 | async-start | bytes 5242880 | tf_op jit(solution)/shard_map/all_gather | solution.py:69
  54.2 245.2 %all-gather.29.cloned.1.call-start = ((), (), s32[]{:S(2)}) async-start(), calls=%async_computation.4 | async-start | bytes 1114112 | tf_op jit(solution)/shard_map/all_gather | solution.py:76
  57.0 245.6 %all-gather.21.cloned.1.call-start = ((), (), s32[]{:S(2)}) async-start(), calls=%async_computation | async-start | bytes 1114112 | tf_op jit(solution)/shard_map/all_gather | solution.py:76
  57.7 280.7 %all-gather.41.cloned.1.call-start = ((), (), s32[]{:S(2)}) async-start(), calls=%async_computation.10 | async-start | bytes 3932160 | tf_op jit(solution)/shard_map/all_gather | solution.py:69
  57.8 18.4 %copy-start.49 = (f32[1,4,1,32,4,1,128]{6,3,4,1,5,2,0:T(8,128)}, f32[1,4,1,32,4,1,128]{6,3,4,1,5,2,0:T(8,128)S(1)}, u32[]{:S(2)}) copy-start(f32[1,4,1,32,4,1,128]{6,3,4,1,5,2,0:T(8,128)S(1)} %copy.144) | copy-start | bytes 786436
  199.0 25.2 %copy-start.63 = (f32[32,4,128]{2,1,0:T(4,128)S(1)}, f32[32,4,128]{2,1,0:T(4,128)}, u32[]{:S(2)}) copy-start(f32[32,4,128]{2,1,0:T(4,128)} %get-tuple-element.76) | copy-start | bytes 196612
  199.0 25.8 %copy-start.62 = (f32[32,4,128]{2,1,0:T(4,128)S(1)}, f32[32,4,128]{2,1,0:T(4,128)}, u32[]{:S(2)}) copy-start(f32[32,4,128]{2,1,0:T(4,128)} %get-tuple-element.199) | copy-start | bytes 196612
  199.0 26.4 %copy-start.61 = (f32[32,4,128]{2,1,0:T(4,128)S(1)}, f32[32,4,128]{2,1,0:T(4,128)}, u32[]{:S(2)}) copy-start(f32[32,4,128]{2,1,0:T(4,128)} %get-tuple-element.75) | copy-start | bytes 196612
  199.0 27.0 %copy-start.60 = (f32[32,4,128]{2,1,0:T(4,128)S(1)}, f32[32,4,128]{2,1,0:T(4,128)}, u32[]{:S(2)}) copy-start(f32[32,4,128]{2,1,0:T(4,128)} %get-tuple-element.197) | copy-start | bytes 196612
  220.4 294.3 %all-gather.31.cloned.1.call-start = ((), (), s32[]{:S(2)}) async-start(), calls=%async_computation.5 | async-start | bytes 1114112 | tf_op jit(solution)/shard_map/all_gather | solution.py:76
  228.1 54.7 %copy-start.8 = (f32[512,512]{1,0:T(8,128)}, f32[512,512]{1,0:T(8,128)S(1)}, u32[]{:S(2)}) copy-start(f32[512,512]{1,0:T(8,128)S(1)} %fusion.39) | copy-start | bytes 3145732
  238.9 39.8 %copy-start.43 = (f32[512,512]{1,0:T(8,128)}, f32[512,512]{1,0:T(8,128)S(1)}, u32[]{:S(2)}) copy-start(f32[512,512]{1,0:T(8,128)S(1)} %get-tuple-element.418) | copy-start | bytes 3145732
  278.2 5.1 copy-start.20
  291.9 6.2 copy-start.67
  299.2 220.4 %all-gather.23.cloned.1.call-start = ((), (), s32[]{:S(2)}) async-start(), calls=%async_computation.1 | async-start | bytes 1114112 | tf_op jit(solution)/shard_map/all_gather | solution.py:76
  302.5 21.1 %copy-start.4 = (f32[512,512]{1,0:T(8,128)}, f32[512,512]{1,0:T(8,128)S(1)}, u32[]{:S(2)}) copy-start(f32[512,512]{1,0:T(8,128)S(1)} %fusion.181) | copy-start | bytes 3145732
  306.0 25.2 %copy-start.6 = (f32[512,512]{1,0:T(8,128)}, f32[512,512]{1,0:T(8,128)S(1)}, u32[]{:S(2)}) copy-start(f32[512,512]{1,0:T(8,128)S(1)} %fusion.182) | copy-start | bytes 3145732
  309.7 9.1 copy-start
  309.7 13.9 %copy-start.64 = (f32[32,4,1,128]{3,0,1,2:T(8,128)}, f32[32,4,1,128]{3,0,1,2:T(8,128)S(1)}, u32[]{:S(2)}) copy-start(f32[32,4,1,128]{3,0,1,2:T(8,128)S(1)} %copy.153) | copy-start | bytes 196612
  338.3 217.1 %all-gather.43.cloned.1.call-start = ((), (), s32[]{:S(2)}) async-start(), calls=%async_computation.11 | async-start | bytes 2621440 | tf_op jit(solution)/shard_map/all_gather | solution.py:69
  349.7 5.5 copy-start.3
  368.1 76.1 %copy-start.71 = (f32[32,2,128]{2,0,1:T(8,128)S(1)}, f32[32,2,128]{2,0,1:T(8,128)}, u32[]{:S(2)}) copy-start(f32[32,2,128]{2,0,1:T(8,128)} %slice_bitcast_fusion.33) | copy-start | bytes 98308
  402.3 107.2 %copy-start.9 = (f32[512,512]{1,0:T(8,128)S(1)}, f32[512,512]{1,0:T(8,128)}, u32[]{:S(2)}) copy-start(f32[512,512]{1,0:T(8,128)} %copy-done.8) | copy-start | bytes 3145732
  462.1 284.1 %all-gather.33.cloned.1.call-start = ((), (), s32[]{:S(2)}) async-start(), calls=%async_computation.6 | async-start | bytes 1114112 | tf_op jit(solution)/shard_map/all_gather | solution.py:76
  470.2 39.8 %copy-start.44 = (f32[512,512]{1,0:T(8,128)}, f32[512,512]{1,0:T(8,128)S(1)}, u32[]{:S(2)}) copy-start(f32[512,512]{1,0:T(8,128)S(1)} %get-tuple-element.419) | copy-start | bytes 3145732
  510.7 13.8 %copy-start.31 = (f32[128,512]{1,0:T(8,128)}, f32[128,512]{1,0:T(8,128)S(1)}, u32[]{:S(2)}) copy-start(f32[128,512]{1,0:T(8,128)S(1)} %fusion.144) | copy-start | bytes 786436
  512.6 11.9 %copy-start.37 = (f32[128,512]{1,0:T(8,128)}, f32[128,512]{1,0:T(8,128)S(1)}, u32[]{:S(2)}) copy-start(f32[128,512]{1,0:T(8,128)S(1)} %fusion.142) | copy-start | bytes 786436
  514.7 9.8 copy-start.42
  518.2 4.8 copy-start.11
  519.6 4.9 copy-start.69
  527.5 226.3 %all-gather.25.cloned.1.call-start = ((), (), s32[]{:S(2)}) async-start(), calls=%async_computation.2 | async-start | bytes 1114112 | tf_op jit(solution)/shard_map/all_gather | solution.py:76
  534.9 7.8 copy-start.70
  537.6 8.1 copy-start.12
  538.7 11.8 %copy-start.68 = (f32[32,3,1,128]{3,0,2,1:T(8,128)}, f32[32,3,1,128]{3,0,2,1:T(8,128)S(1)}, u32[]{:S(2)}) copy-start(f32[32,3,1,128]{3,0,2,1:T(8,128)S(1)} %copy.154) | copy-start | bytes 147460
  545.7 4.8 copy-start.15
  555.3 228.9 %all-gather.45.cloned.1.call-start = ((), (), s32[]{:S(2)}) async-start(), calls=%async_computation.12 | async-start | bytes 1310720 | tf_op jit(solution)/shard_map/all_gather | solution.py:69
  597.4 122.2 %copy-start.73 = (f32[32,1,128]{2,0,1:T(8,128)S(1)}, f32[32,1,128]{2,0,1:T(8,128)}, u32[]{:S(2)}) copy-start(f32[32,1,128]{2,0,1:T(8,128)} %slice_bitcast_fusion.34) | copy-start | bytes 49156
  737.0 206.5 %all-gather.35.cloned.1.call-start = ((), (), s32[]{:S(2)}) async-start(), calls=%async_computation.7 | async-start | bytes 1114112 | tf_op jit(solution)/shard_map/all_gather | solution.py:76
  737.0 5.6 copy-start.58
  746.1 208.8 %all-gather.27.cloned.1.call-start = ((), (), s32[]{:S(2)}) async-start(), calls=%async_computation.3 | async-start | bytes 1114112 | tf_op jit(solution)/shard_map/all_gather | solution.py:76
  771.3 9.7 copy-start.48
  783.8 241.7 %all-reduce.5.cloned.1.call-start = ((), (), s32[]{:S(2)}) async-start(), calls=%async_computation.13 | async-start | bytes 4194304 | tf_op jit(solution)/shard_map/psum | solution.py:97
  786.8 5.8 copy-start.1
  794.5 12.5 %copy-start.22 = (f32[512,512]{0,1:T(8,128)}, f32[512,512]{0,1:T(8,128)S(1)}, u32[]{:S(2)}) copy-start(f32[512,512]{0,1:T(8,128)S(1)} %convolution_subtract_fusion.3) | copy-start | bytes 3145732
  795.1 21.9 %copy-start.45 = (f32[512,512]{1,0:T(8,128)}, f32[512,512]{1,0:T(8,128)S(1)}, u32[]{:S(2)}) copy-start(f32[512,512]{1,0:T(8,128)S(1)} %fusion.31) | copy-start | bytes 3145732
  817.3 117.7 %copy-start.10 = (f32[512,512]{1,0:T(8,128)S(1)}, f32[512,512]{1,0:T(8,128)}, u32[]{:S(2)}) copy-start(f32[512,512]{1,0:T(8,128)} %copy-done.8) | copy-start | bytes 3145732
  894.6 48.9 %copy-start.2 = (f32[512,1024]{1,0:T(8,128)S(1)}, f32[512,1024]{1,0:T(8,128)}, u32[]{:S(2)}) copy-start(f32[512,1024]{1,0:T(8,128)} %fusion.178) | copy-start | bytes 6291460
  935.0 5.3 copy-start.59
  947.7 7.1 copy-start.18
  960.7 5.1 copy-start.23
  965.7 23.0 %copy-start.5 = (f32[512,512]{1,0:T(8,128)S(1)}, f32[512,512]{1,0:T(8,128)}, u32[]{:S(2)}) copy-start(f32[512,512]{1,0:T(8,128)} %copy-done.4) | copy-start | bytes 3145732
  965.7 23.0 %copy-start.13 = (f32[512,512]{1,0:T(8,128)S(1)}, f32[512,512]{1,0:T(8,128)}, u32[]{:S(2)}) copy-start(f32[512,512]{1,0:T(8,128)} %copy-done.11) | copy-start | bytes 3145732
  985.8 4.8 copy-start.7
  1025.5 5.0 copy-start.26
  1025.5 5.1 copy-start.55
  1030.5 10.5 %copy-start.24 = (f32[512,512]{1,0:T(8,128)S(1)}, f32[512,512]{1,0:T(8,128)}, u32[]{:S(2)}) copy-start(f32[512,512]{1,0:T(8,128)} %fusion.175) | copy-start | bytes 3145732
  1030.5 10.5 %copy-start.51 = (f32[1,4,1,32,4,1,128]{6,5,4,3,2,1,0:T(1,128)S(1)}, f32[1,4,1,32,4,1,128]{6,5,4,3,2,1,0:T(1,128)}, u32[]{:S(2)}) copy-start(f32[1,4,1,32,4,1,128]{6,5,4,3,2,1,0:T(1,128)} %param.12) | copy-start | bytes 786436
  1030.5 10.5 %copy-start.52 = (f32[512,128]{0,1:T(8,128)S(1)}, f32[512,128]{0,1:T(8,128)}, u32[]{:S(2)}) copy-start(f32[512,128]{0,1:T(8,128)} %get-tuple-element.121) | copy-start | bytes 786436
  1031.3 9.8 collective-permute-start
  (26 other events, 87.3 us)
Sparse Core Ops, SparseCore 0:
  10.4 41.4 all-gather.36
  54.3 49.2 all-gather.38
  105.5 38.9 all-gather.28
  146.2 37.4 all-gather.20
  220.5 42.9 all-gather.40
  299.3 36.2 all-gather.30
  338.4 36.4 all-gather.22
  462.2 35.6 all-gather.42
  527.6 36.7 all-gather.32
  566.1 37.2 all-gather.24
  737.1 24.4 all-gather.44
  763.3 38.9 all-gather.34
  804.1 37.3 all-gather.26
  963.8 61.6 all-reduce.4
where the time goes:
time: 1060 us; the launch traced here: 1050 us
  other arithmetic  509 us (48%)
  matrix products  188 us (18%)
  local copies, waits for them, and re-layouts  126 us (12%)
  waiting for transfers between devices  109 us (10%)
  blocking collectives  87 us (8%)
  between operations  26.4 us (2%)
    another operation x59, other arithmetic, per_device(): factor = jnp.linalg.cholesky(diagonal_full)  321 us
    another operation x9, other arithmetic, lower_inverse(): lax.linalg.triangular_solve(factor, identity, left_side=True, lower=True)  163 us
    dot_general x27, matrix products, product_tn(): lax.dot_general(left, right, (((0,), (0,)), ((), ())), precision=lax.Prec...  79.9 us
    dot_general x16, matrix products, product(): jnp.dot(left, right, precision=lax.Precision.HIGHEST, preferred_element_t...  60.9 us
    all_gather x3, blocking collectives, gather_block_row(): by_col = lax.all_gather(piece, 'col', axis=0, tiled=True)  56.5 us
    all_gather x1, waiting for transfers between devices, gather_block_row(): by_col = lax.all_gather(piece, 'col', axis=0, tiled=True)  43 us
    another operation x53, local copies, waits for them, and re-layouts, lower_inverse(): lax.linalg.triangular_solve(factor, identity, left_side=True, lower=True)  38.9 us
    psum x1, waiting for transfers between devices, own_columns(): return lax.psum(picked, 'row').reshape(panel_size, panels * col_width)  32.9 us
  transfers between devices with their start and end apart: 15, of which 4 were waited for; matrix products, arithmetic and copies ran while one was open for 76% of the time, Pallas kernels for 0%

commit v1 on v0

--- a/solution.py
+++ b/solution.py
@@ -94,7 +94,9 @@
         spread = solved.reshape(panel_size, panels, row_width)
         picked = lax.dynamic_slice_in_dim(spread, offset, col_width, 2)
         picked = jnp.where(row_index == owner, picked, 0.0)
-        return lax.psum(picked, "row").reshape(panel_size, panels * col_width)
+        return jnp.sum(lax.all_gather(picked, "row"), axis=0).reshape(
+            panel_size, panels * col_width
+        )
 
     factor_blocks = []
     left_solved = []

time: 1060 us -> 1140 us (1.075)
  local copies, waits for them, and re-layouts: 126 us -> 176 us
  other arithmetic: 509 us -> 542 us
  waiting for transfers between devices: 109 us -> 88.7 us
  matrix products: 188 us -> 201 us
    all_gather x0 -> x8, local copies, waits for them, and re-layouts: none -> 37.1 us  [own_columns(): lax.all_gather(picked, 'row')]
    psum x1 -> x0, waiting for transfers between devices: 32.9 us -> none  [own_columns(): return lax.psum(picked, 'row').reshape(panel_size, panels * col_width)]
    reduce_sum x0 -> x8, other arithmetic: none -> 30.9 us  [own_columns(): jnp.sum(lax.all_gather(picked, 'row'), axis=0)]
    all_gather x4, waiting for transfers between devices: 26.8 us -> 45.2 us  [gather_block_row(): whole = lax.all_gather(by_col[:, :, None, :], 'row', axis=2, tiled=True)]
    dot_general x27, matrix products: 79.9 us -> 92.9 us  [product_tn(): lax.dot_general(left, right, (((0,), (0,)), ((), ())), precision=lax.Prec...]
  transfers between devices with their start and end apart: 15 -> 22, of which waited for: 4 -> 2; matrix products, arithmetic and copies ran while one was open for 76% -> 80% of each run, Pallas kernels for 0% -> 0%
where the time goes in v1:
time: 1140 us; the launch traced here: 1130 us
  other arithmetic  542 us (48%)
  matrix products  201 us (18%)
  local copies, waits for them, and re-layouts  176 us (15%)
  waiting for transfers between devices  88.7 us (8%)
  blocking collectives  88.3 us (8%)
  between operations  27 us (2%)
    another operation x59, other arithmetic, per_device(): factor = jnp.linalg.cholesky(diagonal_full)  327 us
    another operation x9, other arithmetic, lower_inverse(): lax.linalg.triangular_solve(factor, identity, left_side=True, lower=True)  161 us
    dot_general x27, matrix products, product_tn(): lax.dot_general(left, right, (((0,), (0,)), ((), ())), precision=lax.Prec...  92.9 us
    dot_general x16, matrix products, product(): jnp.dot(left, right, precision=lax.Precision.HIGHEST, preferred_element_t...  62.1 us
    all_gather x3, blocking collectives, gather_block_row(): by_col = lax.all_gather(piece, 'col', axis=0, tiled=True)  56.3 us
    all_gather x4, waiting for transfers between devices, gather_block_row(): whole = lax.all_gather(by_col[:, :, None, :], 'row', axis=2, tiled=True)  45.2 us
    all_gather x1, waiting for transfers between devices, gather_block_row(): by_col = lax.all_gather(piece, 'col', axis=0, tiled=True)  43 us
    all_gather x8, local copies, waits for them, and re-layouts, own_columns(): lax.all_gather(picked, 'row')  37.1 us
  transfers between devices with their start and end apart: 22, of which 2 were waited for; matrix products, arithmetic and copies ran while one was open for 80% of the time, Pallas kernels for 0%

profile of v1, /device:TPU:8, one launch (start us, length us, event | category | flops | bytes accessed | tf_op | source)
XLA Modules:
  0.0 1128.6 jit_solution(1553343991441988533)
XLA Ops:
  8.8 43.0 %all-gather.53.cloned.1.call-done = f32[1,1,1,512,4,1,128]{6,4,5,2,1,0,3:T(4,128)} async-done(((f32[1,1,1,32,4,1,128]{6,4,5,2,1,0,3:T(4,128)}), f32[1,1,1,512,4,1,128]{6,4,5,2,1,0,3:T(4,128)}) %all-gather.53.cloned.1.call-update) | async-done | bytes 1048592 | tf_op jit(solution)/shard_map/all_gather | solution.py:68
  58.4 45.2 %all-gather.55.cloned.1.call-done = f32[1,1,1,512,4,4,128]{6,3,4,2,1,0,5:T(8,128)} async-done(((f32[1,1,1,512,4,1,128]{6,3,4,2,1,0,5:T(8,128)}), f32[1,1,1,512,4,4,128]{6,3,4,2,1,0,5:T(8,128)}) %all-gather.55.cloned.1.call-update) | async-done | bytes 4194320 | tf_op jit(solution)/shard_map/all_gather | solution.py:69
  103.6 5.4 copy.57
  112.1 11.7 %cholesky.462 = f32[128,128]{1,0:T(8,128)S(1)} custom-call(f32[128,128]{1,0:T(8,128)S(1)} %cholesky.746), custom_call_target="Cholesky" | custom-call | tf_op jit(solution)/shard_map/jit(cholesky)/cholesky | solution.py:114
  124.0 9.8 custom-call.35
  134.5 11.7 %cholesky.481 = f32[128,128]{1,0:T(8,128)S(1)} custom-call(f32[128,128]{1,0:T(8,128)S(1)} %cholesky.750), custom_call_target="Cholesky" | custom-call | tf_op jit(solution)/shard_map/jit(cholesky)/cholesky | solution.py:114
  146.2 10.2 custom-call.36
  157.1 11.7 %cholesky.502 = f32[128,128]{1,0:T(8,128)S(1)} custom-call(f32[128,128]{1,0:T(8,128)S(1)} %cholesky.755), custom_call_target="Cholesky" | custom-call | tf_op jit(solution)/shard_map/jit(cholesky)/cholesky | solution.py:114
  168.9 9.8 custom-call.37
  179.3 11.7 %cholesky.519 = f32[128,128]{1,0:T(8,128)S(1)} custom-call(f32[128,128]{1,0:T(8,128)S(1)} %convolution_subtract_fusion.30), custom_call_target="Cholesky" | custom-call | tf_op jit(solution)/shard_map/jit(cholesky)/cholesky | solution.py:114
  195.9 21.0 %all_gather.107 = f32[512,3,128]{2,0,1:T(8,128)} all-gather(f32[32,3,128]{2,0,1:T(8,128)S(1)} %slice_bitcast_fusion.32), channel_id=1, replica_groups=mesh['tm'=4,'row'=4,'col'=16] {'col'}, dimensions={0}, use_global_device_ids=true | all-gather | bytes 835584 | tf_op jit(solution)/shard_map/all_gather | solution.py:68
  218.5 8.1 while.8
  226.6 39.3 %custom-call.38 = f32[4,128,128]{1,2,0:T(8,128)S(1)} custom-call(f32[4,128,128]{2,1,0:T(8,128)S(1)} %get-tuple-element.52), custom_call_target="InvertDiagBlocksLowerTriangular" | custom-call | tf_op jit(solution)/shard_map/triangular_solve/custom-call.3 | solution.py:19
  281.9 9.0 fusion.183
  292.9 7.1 fusion.4
  303.7 8.0 convolution_subtract_fusion
  319.0 12.5 %cholesky.534 = f32[128,128]{1,0:T(8,128)S(1)} custom-call(f32[128,128]{1,0:T(8,128)} %cholesky.759), custom_call_target="Cholesky" | custom-call | tf_op jit(solution)/shard_map/jit(cholesky)/cholesky | solution.py:114
  331.8 9.8 custom-call.39
  344.1 11.7 %cholesky.553 = f32[128,128]{1,0:T(8,128)S(1)} custom-call(f32[128,128]{1,0:T(8,128)S(1)} %cholesky.763), custom_call_target="Cholesky" | custom-call | tf_op jit(solution)/shard_map/jit(cholesky)/cholesky | solution.py:114
  355.8 10.0 custom-call.40
  367.4 11.7 %cholesky.574 = f32[128,128]{1,0:T(8,128)S(1)} custom-call(f32[128,128]{1,0:T(8,128)S(1)} %cholesky.768), custom_call_target="Cholesky" | custom-call | tf_op jit(solution)/shard_map/jit(cholesky)/cholesky | solution.py:114
  379.2 9.8 custom-call.41
  390.4 11.7 %cholesky.591 = f32[128,128]{1,0:T(8,128)S(1)} custom-call(f32[128,128]{1,0:T(8,128)S(1)} %convolution_subtract_fusion.29), custom_call_target="Cholesky" | custom-call | tf_op jit(solution)/shard_map/jit(cholesky)/cholesky | solution.py:114
  408.4 17.8 %all_gather.109 = f32[512,2,128]{2,1,0:T(2,128)} all-gather(f32[32,2,128]{2,1,0:T(2,128)S(1)} %copy.65), channel_id=1, replica_groups=mesh['tm'=4,'row'=4,'col'=16] {'col'}, dimensions={0}, use_global_device_ids=true | all-gather | bytes 557056 | tf_op jit(solution)/shard_map/all_gather | solution.py:68
  426.4 8.0 while.9
  435.4 39.3 %custom-call.42 = f32[4,128,128]{1,2,0:T(8,128)S(1)} custom-call(f32[4,128,128]{2,1,0:T(8,128)S(1)} %get-tuple-element.53), custom_call_target="InvertDiagBlocksLowerTriangular" | custom-call | tf_op jit(solution)/shard_map/triangular_solve/custom-call.3 | solution.py:19
  487.6 7.9 fusion.2
  505.2 18.2 %all-gather.5 = f32[1,4,1,512,64]{4,1,2,0,3:T(4,128)S(1)} all-gather(f32[1,4,1,32,64]{4,1,2,0,3:T(4,128)S(1)} %copy.77), channel_id=7, replica_groups=mesh['tm'=4,'row'=4,'col'=16] {'col'}, dimensions={3}, use_global_device_ids=true | all-gather | bytes 557056 | tf_op jit(solution)/shard_map/all_gather | solution.py:82
  528.0 6.5 reshape.296
  539.0 4.7 fusion
  543.8 6.8 fusion.7
  550.6 4.6 copy.126
  559.0 4.8 copy.118
  569.8 7.4 fusion.179
  581.4 5.5 fusion.9
  594.6 11.7 %cholesky.606 = f32[128,128]{1,0:T(8,128)S(1)} custom-call(f32[128,128]{1,0:T(8,128)S(1)} %cholesky.772), custom_call_target="Cholesky" | custom-call | tf_op jit(solution)/shard_map/jit(cholesky)/cholesky | solution.py:114
  608.1 9.8 custom-call.43
  621.8 11.7 %cholesky.625 = f32[128,128]{1,0:T(8,128)S(1)} custom-call(f32[128,128]{1,0:T(8,128)S(1)} %cholesky.776), custom_call_target="Cholesky" | custom-call | tf_op jit(solution)/shard_map/jit(cholesky)/cholesky | solution.py:114
  634.7 10.2 custom-call.44
  648.8 13.2 %cholesky.646 = f32[128,128]{1,0:T(8,128)} custom-call(f32[128,128]{1,0:T(8,128)} %cholesky.781), custom_call_target="Cholesky" | custom-call | tf_op jit(solution)/shard_map/jit(cholesky)/cholesky | solution.py:114
  664.0 11.3 custom-call.45
  678.4 11.7 %cholesky.663 = f32[128,128]{1,0:T(8,128)S(1)} custom-call(f32[128,128]{1,0:T(8,128)S(1)} %convolution_subtract_fusion.28), custom_call_target="Cholesky" | custom-call | tf_op jit(solution)/shard_map/jit(cholesky)/cholesky | solution.py:114
  700.5 17.5 %all_gather.111 = f32[512,1,128]{2,0,1:T(8,128)} all-gather(f32[32,1,128]{2,0,1:T(8,128)} %slice_bitcast_fusion.34), channel_id=1, replica_groups=mesh['tm'=4,'row'=4,'col'=16] {'col'}, dimensions={0}, use_global_device_ids=true | all-gather | bytes 278528 | tf_op jit(solution)/shard_map/all_gather | solution.py:68
  730.1 4.8 fusion.14
  734.9 4.8 fusion.12
  741.4 4.8 copy.128
  752.2 4.6 copy.120
  769.0 11.6 %while.10 = (s32[]{:T(128)}, f32[512,512]{1,0:T(8,128)}, s32[4,2]{0,1:T(2,128)S(1)}, f32[4,128,128]{2,1,0:T(8,128)S(1)}, s32[]{:T(128)}) while((s32[]{:T(128)}, f32[512,512]{1,0:T(8,128)}, s32[4,2]{0,1:T(2,128)S(1)}, f32[4,128,128]{2,1,0:T(8,128)S(1)}, s32[]{:T(128)}) %tuple.191), condition=%wide.while_cond.clone.1, body=%wide.while_body.clone.1.sunk | while | flops 2 | bytes 131189 | solution.py:19
  780.5 39.9 %custom-call.46 = f32[4,128,128]{1,2,0:T(8,128)} custom-call(f32[4,128,128]{2,1,0:T(8,128)S(1)} %get-tuple-element.54), custom_call_target="InvertDiagBlocksLowerTriangular" | custom-call | tf_op jit(solution)/shard_map/triangular_solve/custom-call.3 | solution.py:19
  829.6 5.0 fusion.24
  839.3 6.8 fusion.178
  854.0 5.0 fusion.22
  878.8 11.7 %cholesky.678 = f32[128,128]{1,0:T(8,128)S(1)} custom-call(f32[128,128]{1,0:T(8,128)S(1)} %cholesky.785), custom_call_target="Cholesky" | custom-call | tf_op jit(solution)/shard_map/jit(cholesky)/cholesky | solution.py:114
  890.7 10.2 custom-call.47
  902.6 11.7 %cholesky.697 = f32[128,128]{1,0:T(8,128)S(1)} custom-call(f32[128,128]{1,0:T(8,128)S(1)} %cholesky.789), custom_call_target="Cholesky" | custom-call | tf_op jit(solution)/shard_map/jit(cholesky)/cholesky | solution.py:114
  914.3 9.8 custom-call.48
  925.7 11.7 %cholesky.718 = f32[128,128]{1,0:T(8,128)S(1)} custom-call(f32[128,128]{1,0:T(8,128)S(1)} %cholesky.794), custom_call_target="Cholesky" | custom-call | tf_op jit(solution)/shard_map/jit(cholesky)/cholesky | solution.py:114
  937.4 10.0 custom-call.49
  948.8 11.7 %cholesky.735 = f32[128,128]{1,0:T(8,128)S(1)} custom-call(f32[128,128]{1,0:T(8,128)S(1)} %convolution_subtract_fusion.27), custom_call_target="Cholesky" | custom-call | tf_op jit(solution)/shard_map/jit(cholesky)/cholesky | solution.py:114
  965.9 8.0 while.11
  973.9 39.3 %custom-call.50 = f32[4,128,128]{1,2,0:T(8,128)S(1)} custom-call(f32[4,128,128]{2,1,0:T(8,128)S(1)} %get-tuple-element.55), custom_call_target="InvertDiagBlocksLowerTriangular" | custom-call | tf_op jit(solution)/shard_map/triangular_solve/custom-call.3 | solution.py:19
  1072.7 4.6 copy.132
  1077.3 4.6 reduce_sum.88
  1089.1 13.8 %all-gather.14 = f32[256,64]{1,0:T(8,128)S(1)} all-gather(f32[64,64]{1,0:T(8,128)} %convolution_add_fusion.6), channel_id=16, replica_groups=mesh['tm'=4,'row'=4,'col'=16] {'tm'}, dimensions={0}, use_global_device_ids=true | all-gather | bytes 81920 | tf_op jit(solution)/shard_map/all_gather | solution.py:180
  (500 shorter events, 333.8 us)
Async XLA Ops:
  7.2 50.5 %copy-start.59 = (f32[1,4,1,32,4,1,128]{6,5,4,3,2,1,0:T(1,128)S(1)}, f32[1,4,1,32,4,1,128]{6,5,4,3,2,1,0:T(1,128)}, u32[]{:S(2)}) copy-start(f32[1,4,1,32,4,1,128]{6,5,4,3,2,1,0:T(1,128)} %param.9) | copy-start | bytes 786436
  7.2 47.1 %copy-start.65 = (f32[1,4,1,32,4,1,128]{6,5,4,3,2,1,0:T(1,128)S(1)}, f32[1,4,1,32,4,1,128]{6,5,4,3,2,1,0:T(1,128)}, u32[]{:S(2)}) copy-start(f32[1,4,1,32,4,1,128]{6,5,4,3,2,1,0:T(1,128)} %param.11) | copy-start | bytes 786436
  7.2 47.1 %copy-start.66 = (f32[1,4,1,32,4,1,128]{6,5,4,3,2,1,0:T(1,128)S(1)}, f32[1,4,1,32,4,1,128]{6,5,4,3,2,1,0:T(1,128)}, u32[]{:S(2)}) copy-start(f32[1,4,1,32,4,1,128]{6,5,4,3,2,1,0:T(1,128)} %param.10) | copy-start | bytes 786436
  7.2 44.7 %all-gather.53.cloned.1.call-start = ((), (), s32[]{:S(2)}) async-start(), calls=%async_computation.8 | async-start | bytes 1114112 | tf_op jit(solution)/shard_map/all_gather | solution.py:68
  8.8 94.8 %all-gather.55.cloned.1.call-start = ((), (), s32[]{:S(2)}) async-start(), calls=%async_computation.9 | async-start | bytes 5242880 | tf_op jit(solution)/shard_map/all_gather | solution.py:69
  54.2 215.9 %all-gather.37.cloned.1.call-start = ((), (), s32[]{:S(2)}) async-start(), calls=%async_computation | async-start | bytes 1114112 | tf_op jit(solution)/shard_map/all_gather | solution.py:76
  56.9 218.9 %all-gather.45.cloned.1.call-start = ((), (), s32[]{:S(2)}) async-start(), calls=%async_computation.4 | async-start | bytes 1114112 | tf_op jit(solution)/shard_map/all_gather | solution.py:76
  57.6 242.5 %all-gather.57.cloned.1.call-start = ((), (), s32[]{:S(2)}) async-start(), calls=%async_computation.10 | async-start | bytes 3932160 | tf_op jit(solution)/shard_map/all_gather | solution.py:69
  216.9 264.0 %all-gather.39.cloned.1.call-start = ((), (), s32[]{:S(2)}) async-start(), calls=%async_computation.1 | async-start | bytes 1114112 | tf_op jit(solution)/shard_map/all_gather | solution.py:76
  218.2 277.2 %all-gather.47.cloned.1.call-start = ((), (), s32[]{:S(2)}) async-start(), calls=%async_computation.5 | async-start | bytes 1114112 | tf_op jit(solution)/shard_map/all_gather | solution.py:76
  218.4 50.4 %copy-start.10 = (f32[512,512]{1,0:T(8,128)}, f32[512,512]{1,0:T(8,128)S(1)}, u32[]{:S(2)}) copy-start(f32[512,512]{1,0:T(8,128)S(1)} %fusion.39) | copy-start | bytes 3145732
  266.0 284.6 %all-gather.71.cloned.1.call-start = ((), (), s32[]{:S(2)}) async-start(), calls=%async_computation.17 | async-start | bytes 1310720 | tf_op jit(solution)/shard_map/all_gather | solution.py:97
  267.2 14.7 %copy-start.27 = (f32[128,512]{1,0:T(8,128)}, f32[128,512]{1,0:T(8,128)S(1)}, u32[]{:S(2)}) copy-start(f32[128,512]{1,0:T(8,128)S(1)} %fusion.150) | copy-start | bytes 786436
  268.1 13.8 %copy-start.35 = (f32[128,512]{1,0:T(8,128)}, f32[128,512]{1,0:T(8,128)S(1)}, u32[]{:S(2)}) copy-start(f32[128,512]{1,0:T(8,128)S(1)} %fusion.148) | copy-start | bytes 786436
  270.1 11.9 %copy-start.43 = (f32[128,512]{1,0:T(8,128)}, f32[128,512]{1,0:T(8,128)S(1)}, u32[]{:S(2)}) copy-start(f32[128,512]{1,0:T(8,128)S(1)} %fusion.147) | copy-start | bytes 786436
  273.2 17.7 %copy-start.4 = (f32[512,512]{1,0:T(8,128)}, f32[512,512]{1,0:T(8,128)S(1)}, u32[]{:S(2)}) copy-start(f32[512,512]{1,0:T(8,128)S(1)} %fusion.182) | copy-start | bytes 3145732
  274.3 284.6 %all-gather.63.cloned.1.call-start = ((), (), s32[]{:S(2)}) async-start(), calls=%async_computation.13 | async-start | bytes 1310720 | tf_op jit(solution)/shard_map/all_gather | solution.py:97
  278.8 12.1 %copy-start.7 = (f32[512,512]{1,0:T(8,128)}, f32[512,512]{1,0:T(8,128)S(1)}, u32[]{:S(2)}) copy-start(f32[512,512]{1,0:T(8,128)S(1)} %fusion.181) | copy-start | bytes 3145732
  300.0 277.2 %all-gather.59.cloned.1.call-start = ((), (), s32[]{:S(2)}) async-start(), calls=%async_computation.11 | async-start | bytes 2621440 | tf_op jit(solution)/shard_map/all_gather | solution.py:69
  365.8 108.9 %copy-start.11 = (f32[512,512]{1,0:T(8,128)S(1)}, f32[512,512]{1,0:T(8,128)}, u32[]{:S(2)}) copy-start(f32[512,512]{1,0:T(8,128)} %copy-done.10) | copy-start | bytes 3145732
  426.3 315.1 %all-gather.73.cloned.1.call-start = ((), (), s32[]{:S(2)}) async-start(), calls=%async_computation.18 | async-start | bytes 1310720 | tf_op jit(solution)/shard_map/all_gather | solution.py:97
  475.1 20.3 %copy-start.25 = (f32[128,512]{1,0:T(8,128)}, f32[128,512]{1,0:T(8,128)S(1)}, u32[]{:S(2)}) copy-start(f32[128,512]{1,0:T(8,128)S(1)} %fusion.90) | copy-start | bytes 786436
  476.8 18.6 %copy-start.29 = (f32[128,512]{1,0:T(8,128)}, f32[128,512]{1,0:T(8,128)S(1)}, u32[]{:S(2)}) copy-start(f32[128,512]{1,0:T(8,128)S(1)} %fusion.144) | copy-start | bytes 786436
  478.7 16.8 %copy-start.37 = (f32[128,512]{1,0:T(8,128)}, f32[128,512]{1,0:T(8,128)S(1)}, u32[]{:S(2)}) copy-start(f32[128,512]{1,0:T(8,128)S(1)} %fusion.142) | copy-start | bytes 786436
  480.8 14.7 %copy-start.45 = (f32[128,512]{1,0:T(8,128)}, f32[128,512]{1,0:T(8,128)S(1)}, u32[]{:S(2)}) copy-start(f32[128,512]{1,0:T(8,128)S(1)} %fusion.141) | copy-start | bytes 786436
  480.8 6.7 copy-start.8
  484.4 11.1 copy-start.13
  487.5 264.6 %all-gather.65.cloned.1.call-start = ((), (), s32[]{:S(2)}) async-start(), calls=%async_computation.14 | async-start | bytes 1310720 | tf_op jit(solution)/shard_map/all_gather | solution.py:97
  498.9 25.3 %copy-start.16 = (f32[512,512]{1,0:T(8,128)}, f32[512,512]{1,0:T(8,128)S(1)}, u32[]{:S(2)}) copy-start(f32[512,512]{1,0:T(8,128)S(1)} %fusion.23) | copy-start | bytes 3145732
  500.1 329.5 %all-gather.41.cloned.1.call-start = ((), (), s32[]{:S(2)}) async-start(), calls=%async_computation.2 | async-start | bytes 1114112 | tf_op jit(solution)/shard_map/all_gather | solution.py:76
  527.9 326.2 %all-gather.49.cloned.1.call-start = ((), (), s32[]{:S(2)}) async-start(), calls=%async_computation.6 | async-start | bytes 1114112 | tf_op jit(solution)/shard_map/all_gather | solution.py:76
  528.0 8.2 copy-start.28
  528.0 8.2 copy-start.36
  528.0 8.2 copy-start.44
  535.5 8.3 copy-start.64
  563.8 6.0 copy-start.26
  577.2 290.7 %all-gather.61.cloned.1.call-start = ((), (), s32[]{:S(2)}) async-start(), calls=%async_computation.12 | async-start | bytes 1310720 | tf_op jit(solution)/shard_map/all_gather | solution.py:69
  718.0 304.7 %all-gather.43.cloned.1.call-start = ((), (), s32[]{:S(2)}) async-start(), calls=%async_computation.3 | async-start | bytes 1114112 | tf_op jit(solution)/shard_map/all_gather | solution.py:76
  739.7 297.7 %all-gather.51.cloned.1.call-start = ((), (), s32[]{:S(2)}) async-start(), calls=%async_computation.7 | async-start | bytes 1114112 | tf_op jit(solution)/shard_map/all_gather | solution.py:76
  820.5 227.7 %all-gather.75.cloned.1.call-start = ((), (), s32[]{:S(2)}) async-start(), calls=%async_computation.19 | async-start | bytes 1310720 | tf_op jit(solution)/shard_map/all_gather | solution.py:97
  820.6 5.6 copy-start.62
  838.9 218.5 %all-gather.67.cloned.1.call-start = ((), (), s32[]{:S(2)}) async-start(), calls=%async_computation.15 | async-start | bytes 1310720 | tf_op jit(solution)/shard_map/all_gather | solution.py:97
  867.7 205.0 %all-gather.77.cloned.1.call-start = ((), (), s32[]{:S(2)}) async-start(), calls=%async_computation.20 | async-start | bytes 1310720 | tf_op jit(solution)/shard_map/all_gather | solution.py:97
  870.5 5.8 copy-start.1
  878.2 12.5 %copy-start.21 = (f32[512,512]{0,1:T(8,128)}, f32[512,512]{0,1:T(8,128)S(1)}, u32[]{:S(2)}) copy-start(f32[512,512]{0,1:T(8,128)S(1)} %convolution_subtract_fusion.3) | copy-start | bytes 3145732
  878.7 22.1 %copy-start.53 = (f32[512,512]{1,0:T(8,128)}, f32[512,512]{1,0:T(8,128)S(1)}, u32[]{:S(2)}) copy-start(f32[512,512]{1,0:T(8,128)S(1)} %fusion.31) | copy-start | bytes 3145732
  901.2 112.1 %copy-start.12 = (f32[512,512]{1,0:T(8,128)S(1)}, f32[512,512]{1,0:T(8,128)}, u32[]{:S(2)}) copy-start(f32[512,512]{1,0:T(8,128)} %copy-done.10) | copy-start | bytes 3145732
  973.9 40.6 %copy-start.50 = (f32[512,512]{1,0:T(8,128)}, f32[512,512]{1,0:T(8,128)S(1)}, u32[]{:S(2)}) copy-start(f32[512,512]{1,0:T(8,128)S(1)} %get-tuple-element.405) | copy-start | bytes 3145732
  1014.5 8.0 copy-start.30
  1014.9 7.8 copy-start.2
  1016.4 6.2 copy-start.38
  1026.9 8.4 copy-start.69
  1027.0 9.3 copy-start.68
  1027.0 9.3 copy-start.70
  1027.0 10.4 copy-start.19
  1035.1 75.3 %all-gather.69.cloned.1.call-start = ((), (), s32[]{:S(2)}) async-start(), calls=%async_computation.16 | async-start | bytes 1310720 | tf_op jit(solution)/shard_map/all_gather | solution.py:97
  1043.2 9.6 copy-start.23
  1061.9 7.7 copy-start.18
  1061.9 7.7 copy-start.54
  1077.3 6.8 copy-start.22
  1077.3 27.7 %copy-start.6 = (f32[512,512]{1,0:T(8,128)S(1)}, f32[512,512]{1,0:T(8,128)}, u32[]{:S(2)}) copy-start(f32[512,512]{1,0:T(8,128)} %copy-done.4) | copy-start | bytes 3145732
  1077.3 27.7 %copy-start.15 = (f32[512,512]{1,0:T(8,128)S(1)}, f32[512,512]{1,0:T(8,128)}, u32[]{:S(2)}) copy-start(f32[512,512]{1,0:T(8,128)} %copy-done.13) | copy-start | bytes 3145732
  1086.5 21.9 %copy-start.9 = (f32[512,512]{1,0:T(8,128)S(1)}, f32[512,512]{1,0:T(8,128)}, u32[]{:S(2)}) copy-start(f32[512,512]{1,0:T(8,128)} %copy-done.7) | copy-start | bytes 3145732
  1086.5 32.3 %collective-permute-start = (f32[128,512]{1,0:T(8,128)}, f32[128,512]{1,0:T(8,128)}, u32[]{:S(2)}, u32[]{:S(2)}) collective-permute-start(f32[128,512]{1,0:T(8,128)} %convolution_add_fusion), channel_id=1, source_target_pairs={{64,0},{128,64},{192,128},{65,1},{129,65},{193,129},{66,2},{130,66... | collective-permute-start | bytes 786440 | tf_op jit(solution)/shard_map/ppermute | solution.py:10
  (30 other events, 100.7 us)
Sparse Core Ops, SparseCore 0:
  10.4 41.4 all-gather.52
  54.3 49.2 all-gather.54
  106.0 39.0 all-gather.36
  147.3 37.6 all-gather.44
  217.0 43.3 all-gather.56
  262.1 38.8 all-gather.38
  302.8 37.2 all-gather.46
  341.9 25.3 all-gather.70
  369.1 27.4 all-gather.62
  426.4 35.5 all-gather.58
  487.6 24.8 all-gather.72
  514.2 27.0 all-gather.64
  543.0 38.9 all-gather.40
  583.7 37.3 all-gather.48
  718.1 24.7 all-gather.60
  744.6 39.0 all-gather.42
  820.6 36.7 all-gather.50
  859.1 25.1 all-gather.74
  886.1 27.2 all-gather.66
  1035.2 24.8 all-gather.76
  1062.0 26.9 all-gather.68
